TPU v7x, 32 devices: a whole 2x2x4 slice. The times are simulated.
32 devices in a mesh: dp: 4 (over x, core), mp: 8 (over z, y).
Axes of the slice: x: 2, y: 2, z: 4, core: 2. Of those that a mesh axis runs over, the one named last changes fastest.
Arguments:
- queries: bfloat16 [512, 4096], P('dp'), may hold values from -103 to 103
- new_kv: bfloat16 [2, 512, 1024], P(None, 'dp'), may hold values from -6 to 6
- residual: bfloat16 [512, 4096], P('dp', 'mp'), may hold values from -2.4 to 2.4
- out_weight: bfloat16 [4096, 4096], P('mp'), may hold values from -0.125 to 0.125
- norm_gain: float32 [4096], replicated, may hold values from 0.5 to 1.5
- router: bfloat16 [4096, 8], replicated, may hold values from -0.09375 to 0.09375
- expert_in: bfloat16 [8, 2, 8192, 4096], P('dp', None, 'mp'), may hold values from -0.09375 to 0.09375
- expert_out: bfloat16 [8, 8192, 4096], P('dp', 'mp'), may hold values from -0.09375 to 0.09375
- node_cache: bfloat16 [2, 384, 8, 128, 128], P(None, 'dp', 'mp'), may hold values from -6 to 6
- leaf_cache: bfloat16 [2, 512, 8, 128, 128], P(None, 'dp', 'mp'), may hold values from -6 to 6
- slot_request: int32 [512], replicated, may hold values from 0 to 511, each once
- request_branch: int32 [512], replicated, may hold values from 0 to 31, as said below
- branch_parent: int32 [32], replicated, may hold values from 0 to 7, as said below
- root_owner: int32 [8], replicated, may hold values from 0 to 3, as said below
- branch_owner: int32 [32], replicated, may hold values from 0 to 3, as said below
- root_pages: int32 [8, 32], replicated, may hold values from 0 to 95, as said below
- branch_pages: int32 [32, 4], replicated, may hold values from 0 to 95, as said below
- root_len: int32 [8], replicated, may hold values from 1 to 4096, as said below
- branch_len: int32 [32], replicated, may hold values from 1 to 512
- leaf_len: int32 [512], P('dp'), may hold values from 1 to 128
- routes: int32 [512, 2], P('dp'), may hold values from 0 to 7, all different within a row; in each aligned block of 128 rows (0 to 127, 128 to 255, ...) at most 64 rows name the same one
Outputs:
- layer_out: bfloat16 [512, 4096], P('dp', 'mp')
Inputs may be any that keep to these rules, and one draw needn't show every extreme that they name: `request_branch`: at most 32 requests share a branch, and some branch has exactly 32. `branch_parent`: every root has exactly 4 branches. `root_owner`: every index of dp holds exactly 2 roots. `branch_owner`: every index of dp holds exactly 8 branches. `root_pages`: no slot of an owner's pool serves two pages of its nodes. `branch_pages`: no slot of an owner's pool serves two pages of its nodes. `root_len`: some root has 32 full pages.
All inputs are finite; a program needn't handle non-finite values.
Results may differ from a plain program's by a relative error of at most 0.034.
Values may be sent and summed in bfloat16 or wider, within the bound.
No kernel may reach another device: no remote copies, remote signals or barrier semaphores. Data moves between devices by JAX's collectives and lax.ppermute only.
A program may use at most 576 MiB of HBM per device.

v0:
```python
import jax
import jax.numpy as jnp
from jax import lax
from jax.sharding import PartitionSpec as P

HEADS = 32
KVH = 8
EXPERTS = 8
TOP = 2
PAGE = 128
ROOT_DEV = 2
BR_DEV = 8
BR_CAP = 32
E_CAP = 64
MASKED_SCORE = -1e30
NORM_EPS = 1e-05


def partner(x, axis, apart):
    return lax.ppermute(x, axis, [(i, i ^ 1 << apart) for i in range(lax.axis_size(axis))])


def merge_partials(first_part, second_part):
    first_sum, first_max, first_total = first_part
    second_sum, second_max, second_total = second_part
    common_max = jnp.maximum(first_max, second_max)
    first_factor = jnp.exp(first_max - common_max)
    second_factor = jnp.exp(second_max - common_max)
    merged_sum = first_sum * first_factor[..., None] + second_sum * second_factor[..., None]
    return (merged_sum, common_max, first_total * first_factor + second_total * second_factor)


def weigh_scores(scores, usable, values, pattern):
    masked_scores = jnp.where(usable, scores, MASKED_SCORE)
    row_max = jnp.max(masked_scores, axis=-1)
    weights = jnp.where(usable, jnp.exp(masked_scores - row_max[..., None]), 0.0)
    weight_total = jnp.sum(weights, axis=-1)
    weighted_sum = jnp.einsum(
        pattern, weights.astype(jnp.bfloat16), values, preferred_element_type=jnp.float32
    )
    return (weighted_sum, row_max, weight_total)


def node_partial(all_queries, members, page_pool, page_list, node_length, part_index):
    token_width = page_pool.shape[2]
    head_width = page_pool.shape[3]
    query_rows = jnp.take(all_queries, members, axis=0, mode="fill", fill_value=0)
    node_block = jnp.take(page_pool, page_list, axis=1)
    node_keys = node_block[0].reshape(-1, head_width)
    node_values = node_block[1].reshape(-1, head_width)
    positions = (
        jnp.arange(page_list.shape[0])[:, None] * PAGE
        + part_index * token_width
        + jnp.arange(token_width)[None, :]
    ).reshape(-1)
    usable = (positions < node_length)[None, None, :]
    scores = jnp.einsum(
        "sgd,ld->sgl", query_rows, node_keys, preferred_element_type=jnp.float32
    ) * head_width ** (-0.5)
    return weigh_scores(scores, usable, node_values, "sgl,ld->sgd")


def spread_rows(member_ids, partial_value, requests):
    weighted_sum, row_max, weight_total = partial_value
    flat_ids = member_ids.reshape(-1)
    groups = row_max.shape[-1]
    head_width = weighted_sum.shape[-1]
    sum_rows = (
        jnp.zeros((requests, groups, head_width), jnp.float32)
        .at[flat_ids]
        .set(weighted_sum.reshape(-1, groups, head_width), mode="drop")
    )
    max_rows = (
        jnp.zeros((requests, groups), jnp.float32)
        .at[flat_ids]
        .set(row_max.reshape(-1, groups), mode="drop")
    )
    total_rows = (
        jnp.zeros((requests, groups), jnp.float32)
        .at[flat_ids]
        .set(weight_total.reshape(-1, groups), mode="drop")
    )
    return (sum_rows, max_rows, total_rows)


def shards(
    queries,
    new_kv,
    residual,
    out_weight,
    norm_gain,
    router,
    expert_in,
    expert_out,
    node_cache,
    leaf_cache,
    slot_request,
    request_branch,
    branch_parent,
    root_owner,
    branch_owner,
    root_pages,
    branch_pages,
    root_len,
    branch_len,
    leaf_len,
    routes,
):
    head_width = node_cache.shape[-1]
    token_width = node_cache.shape[-2]
    part_count = lax.axis_size("mp") // KVH
    group_size = HEADS // KVH
    own_heads = HEADS // lax.axis_size("mp")
    local_rows = queries.shape[0]
    requests = slot_request.shape[0]
    branches = branch_parent.shape[0]
    root_count = root_owner.shape[0]
    kid_count = branches // root_count
    mp_index = lax.axis_index("mp")
    dp_index = lax.axis_index("dp")
    kv_head = mp_index // part_count
    part_index = mp_index % part_count
    group_queries = lax.dynamic_slice_in_dim(
        queries, kv_head * group_size * head_width, group_size * head_width, 1
    )
    all_queries = lax.all_gather(group_queries, "dp", axis=0, tiled=True).reshape(
        requests, group_size, head_width
    )
    slot_branch = jnp.take(request_branch, slot_request)
    branch_order = jnp.argsort(slot_branch, stable=True)
    branch_counts = jnp.sum(
        (slot_branch[None, :] == jnp.arange(branches)[:, None]).astype(jnp.int32), axis=1
    )
    branch_starts = jnp.cumsum(branch_counts) - branch_counts
    offsets = jnp.arange(BR_CAP)[None, :]
    spots = jnp.minimum(branch_starts[:, None] + offsets, requests - 1)
    members = jnp.where(offsets < branch_counts[:, None], jnp.take(branch_order, spots), requests)
    kids_of = jnp.argsort(branch_parent, stable=True).reshape(root_count, kid_count)
    page_pool = node_cache[:, :, 0]
    local_roots = jnp.nonzero(root_owner == dp_index, size=ROOT_DEV)[0]
    local_branches = jnp.nonzero(branch_owner == dp_index, size=BR_DEV)[0]

    def root_work(root_node):
        member_ids = jnp.take(members, kids_of[root_node], axis=0).reshape(-1)
        return (
            member_ids,
            node_partial(
                all_queries,
                member_ids,
                page_pool,
                root_pages[root_node],
                root_len[root_node],
                part_index,
            ),
        )

    def branch_work(branch_node):
        member_ids = members[branch_node]
        return (
            member_ids,
            node_partial(
                all_queries,
                member_ids,
                page_pool,
                branch_pages[branch_node],
                branch_len[branch_node],
                part_index,
            ),
        )

    root_ids, root_partial = jax.vmap(root_work)(local_roots)
    branch_ids, branch_partial = jax.vmap(branch_work)(local_branches)
    root_sum, root_max, root_total = spread_rows(root_ids, root_partial, requests)
    branch_sum, branch_max, branch_total = spread_rows(branch_ids, branch_partial, requests)
    returned = (
        lax.psum_scatter(root_sum, "dp", scatter_dimension=0, tiled=True),
        lax.psum_scatter(root_max, "dp", scatter_dimension=0, tiled=True),
        lax.psum_scatter(root_total, "dp", scatter_dimension=0, tiled=True),
        lax.psum_scatter(branch_sum, "dp", scatter_dimension=0, tiled=True),
        lax.psum_scatter(branch_max, "dp", scatter_dimension=0, tiled=True),
        lax.psum_scatter(branch_total, "dp", scatter_dimension=0, tiled=True),
    )
    leaf_block = leaf_cache[:, :, 0]
    mine_queries = group_queries.reshape(local_rows, group_size, head_width)
    leaf_places = part_index * token_width + jnp.arange(token_width)
    leaf_usable = (leaf_places[None, :] < leaf_len[:, None])[:, None, :]
    leaf_scores = jnp.einsum(
        "rgd,rtd->rgt", mine_queries, leaf_block[0], preferred_element_type=jnp.float32
    ) * head_width ** (-0.5)
    leaf_partial = weigh_scores(leaf_scores, leaf_usable, leaf_block[1], "rgt,rtd->rgd")
    running = merge_partials(
        (returned[0], returned[1], returned[2]), (returned[3], returned[4], returned[5])
    )
    running = merge_partials(running, leaf_partial)
    bit_count = part_count.bit_length() - 1
    for bit_index in reversed(range(bit_count)):
        half_heads = running[1].shape[1] // 2
        upper_side = mp_index >> bit_index & 1 == 1
        kept_half = tuple(
            (
                jnp.where(upper_side, component[:, half_heads:], component[:, :half_heads])
                for component in running
            )
        )
        sent_half = tuple(
            (
                jnp.where(upper_side, component[:, :half_heads], component[:, half_heads:])
                for component in running
            )
        )
        received = partner((sent_half[0], sent_half[1], sent_half[2]), "mp", bit_index)
        running = merge_partials(kept_half, received)
    own_queries = lax.dynamic_slice_in_dim(
        queries, mp_index * own_heads * head_width, own_heads * head_width, 1
    ).reshape(local_rows, own_heads, head_width)
    fresh_kv = lax.dynamic_slice_in_dim(new_kv, kv_head * head_width, head_width, 2)
    self_score = jnp.einsum(
        "rhd,rd->rh", own_queries, fresh_kv[0], preferred_element_type=jnp.float32
    ) * head_width ** (-0.5)
    weighted, row_max, weight_total = running
    common_max = jnp.maximum(row_max, self_score)
    old_factor = jnp.exp(row_max - common_max)
    new_factor = jnp.exp(self_score - common_max)
    weighted = (
        weighted * old_factor[..., None]
        + new_factor[..., None] * fresh_kv[1].astype(jnp.float32)[:, None, :]
    )
    weight_total = weight_total * old_factor + new_factor
    attended = (
        (weighted / weight_total[..., None])
        .astype(jnp.bfloat16)
        .reshape(local_rows, own_heads * head_width)
    )
    projected = jnp.dot(attended, out_weight, preferred_element_type=jnp.float32)
    slice_width = residual.shape[1]
    start_col = mp_index * slice_width
    own_cols = lax.dynamic_slice_in_dim(projected, start_col, slice_width, 1) + residual.astype(
        jnp.float32
    )
    projected = lax.dynamic_update_slice_in_dim(projected, own_cols, start_col, 1)
    hidden = lax.psum(projected.astype(jnp.bfloat16), "mp").astype(jnp.float32)
    inv_rms = lax.rsqrt(jnp.mean(hidden * hidden, axis=1) + NORM_EPS)
    normed = (hidden * inv_rms[:, None] * norm_gain[None, :]).astype(jnp.bfloat16)
    kept_cols = lax.dynamic_slice_in_dim(hidden, start_col, slice_width, 1)
    logits = jnp.dot(normed, router, preferred_element_type=jnp.float32)
    route_hits = routes[:, :, None] == jnp.arange(EXPERTS)[None, None, :]
    chosen = jnp.sum(jnp.where(route_hits, logits[:, None, :], 0.0), axis=2)
    gate_weights = jax.nn.softmax(chosen, axis=1)
    pair_experts = routes.reshape(-1)
    pair_onehot = (pair_experts[:, None] == jnp.arange(EXPERTS)[None, :]).astype(jnp.int32)
    pair_rank = jnp.sum((jnp.cumsum(pair_onehot, axis=0) - 1) * pair_onehot, axis=1)
    pair_slot = pair_experts * E_CAP + pair_rank
    slot_source = (
        jnp.full((EXPERTS * E_CAP,), local_rows, jnp.int32)
        .at[pair_slot]
        .set(jnp.arange(pair_experts.shape[0], dtype=jnp.int32) // TOP)
    )
    padded = jnp.concatenate([normed, jnp.zeros((1, normed.shape[1]), jnp.bfloat16)], axis=0)
    dp_count = lax.axis_size("dp")
    local_experts = expert_in.shape[0]
    outgoing = jnp.take(padded, slot_source, axis=0).reshape(
        dp_count, local_experts * E_CAP, normed.shape[1]
    )
    incoming = lax.all_to_all(outgoing, "dp", split_axis=0, concat_axis=0, tiled=True).reshape(
        dp_count, local_experts, E_CAP, normed.shape[1]
    )
    gate_up = jnp.einsum(
        "sjcd,jkfd->ksjcf", incoming, expert_in, preferred_element_type=jnp.float32
    )
    expert_hidden = (jax.nn.silu(gate_up[0]) * gate_up[1]).astype(jnp.bfloat16)
    expert_partial = jnp.einsum(
        "sjcf,jfd->sjcd", expert_hidden, expert_out, preferred_element_type=jnp.float32
    )
    summed = lax.psum_scatter(
        expert_partial.astype(jnp.bfloat16), "mp", scatter_dimension=3, tiled=True
    )
    returned_rows = lax.all_to_all(
        summed.reshape(dp_count, local_experts * E_CAP, slice_width),
        "dp",
        split_axis=0,
        concat_axis=0,
        tiled=True,
    )
    results = jnp.take(returned_rows.reshape(-1, slice_width), pair_slot, axis=0).reshape(
        local_rows, TOP, slice_width
    )
    layer_out = kept_cols + jnp.sum(gate_weights[:, :, None] * results.astype(jnp.float32), axis=1)
    return layer_out.astype(jnp.bfloat16)


def solution(mesh):
    placed = (
        P("dp", None),
        P(None, "dp", None),
        P("dp", "mp"),
        P("mp", None),
        P(),
        P(),
        P("dp", None, "mp", None),
        P("dp", "mp", None),
        P(None, "dp", "mp", None, None),
        P(None, "dp", "mp", None, None),
        P(),
        P(),
        P(),
        P(),
        P(),
        P(),
        P(),
        P(),
        P(),
        P("dp"),
        P("dp", None),
    )
    return jax.shard_map(
        shards, mesh=mesh, in_specs=placed, out_specs=P("dp", "mp"), check_vma=False
    )
```

profile of v0, /device:TPU:0, one launch (start us, length us, event | category | flops | bytes accessed | tf_op | source)
XLA Modules:
  0.0 496.6 jit_solution(14215773157432627096)
XLA Ops:
  6.5 0.7 fusion.84
  7.3 1.4 fusion.85
  8.8 0.6 scatter_custom_fusion
  9.6 2.3 sort.34
  12.0 0.7 shift-left_bitcast_fusion.1
  13.3 0.7 compare_select_fusion.11
  14.0 3.6 gather_fusion.1
  17.6 0.7 and_select_fusion.2
  18.8 3.8 sort.35
  22.6 6.9 %gather_fusion.2 = s32[1024]{0:T(1024)S(1)} fusion(s32[512]{0:T(512)S(1)} %get-tuple-element.8, s32[1024]{0:T(1024)S(1)} %broadcast_clamp_fusion), kind=kCustom, calls=%fused_computation.2 | custom fusion | bytes 12288 | tf_op jit(solution)/shard_map/jit(_take)/gather | solution.py:137
  31.3 8.6 %all_gather.3 = bf16[512,512]{1,0:T(8,128)(2,1)S(1)} all-gather(bf16[128,512]{1,0:T(8,128)(2,1)S(1)} %constant_dynamic-slice_fusion), channel_id=1, replica_groups=mesh['dp'=4,'mp'=8] {'dp'}, dimensions={0}, use_global_device_ids=true | all-gather | bytes 655360 | tf_op jit(solution)/shard_map/all_gather | solution.py:126
  40.0 1.0 gather_fusion.5
  41.1 5.8 %gather_fusion.7 = bf16[64,2,128,128]{3,2,1,0:T(8,128)(2,1)} fusion(bf16[2,96,128,128]{3,2,1,0:T(8,128)(2,1)} %bitcast.188, s32[1024]{0:T(1024)S(1)} %pad_clamp_fusion.5), kind=kCustom, calls=%fused_computation.7 | custom fusion | bytes 8388864 | tf_op jit(solution)/shard_map/vmap(jit(_take))/gather | solution.py:48
  46.9 2.6 fusion.18
  49.6 1.8 fusion.96
  51.5 0.6 gather_fusion.4
  52.2 3.0 fusion.4
  55.2 7.2 %fusion.5 = (f32[2,128,4]{1,2,0:T(4,128)S(1)}, bf16[2,128,4,4096]{3,1,2,0:T(8,128)(2,1)}) fusion(f32[2,128,4,4096]{3,1,2,0:T(8,128)S(1)} %get-tuple-element.35, f32[2,128,4]{1,2,0:T(4,128)S(1)} %get-tuple-element.34, pred[2,4096]{1,0:T(4,128)(4,1)S(1)} %broadcast_compare_fusion), kind=kLoop, calls=%fused_computation.31 | loop fusion | flops 25164800 | bytes 25182208 | tf_op jit(solution)/shard_map/vmap()/reduce_sum | solution.py:37
  62.6 1.8 scatter_custom_fusion.6
  64.5 0.6 fusion.87
  65.4 0.9 scatter_custom_fusion.3
  66.5 0.7 shift-left_bitcast_fusion
  69.1 1.0 gather_fusion.10
  70.4 3.8 gather_fusion.12
  75.9 0.6 gather_fusion.9
  76.6 0.6 fusion.27
  77.2 0.8 fusion.28
  78.2 1.8 scatter_custom_fusion.7
  80.2 1.8 scatter_custom_fusion.2
  82.3 1.8 scatter_custom_fusion.4
  84.2 6.3 %fusion.7 = f32[2,128,4,128]{3,1,0,2:T(8,128)S(1)} fusion(bf16[2,4096,128,1]{2,1,0,3:T(8,128)(2,1)} %bitcast.194, bf16[2,128,4,4096]{3,1,2,0:T(8,128)(2,1)} %get-tuple-element.23), kind=kOutput, calls=%fused_computation.33 | convolution fusion | flops 1073741824 | bytes 11010048 | tf_op jit(solution)/shard_map/vmap(sgl,ld->sgd)/dot_general | solution.py:38
  91.8 7.3 %scatter_fusion = f32[512,4,128]{2,1,0:T(4,128)S(1)} fusion(f32[512,4,128]{2,1,0:T(4,128)S(1)} %broadcast.675.clone.1, s32[256]{0:T(256)S(1)} %bitcast.213, f32[256,4,128]{2,1,0:T(4,128)S(1)} %copy.278), kind=kCustom, calls=%fused_computation.16 | custom fusion | bytes 1573888 | tf_op jit(solution)/shard_map/scatter | solution.py:71
  99.2 7.3 %scatter_fusion.1 = f32[512,4,128]{2,1,0:T(4,128)S(1)} fusion(f32[512,4,128]{2,1,0:T(4,128)S(1)} %broadcast.675.clone, s32[256]{0:T(256)S(1)} %bitcast.210, f32[256,4,128]{2,1,0:T(4,128)S(1)} %copy.293), kind=kCustom, calls=%fused_computation.20 | custom fusion | bytes 1573888 | tf_op jit(solution)/shard_map/scatter | solution.py:71
  106.6 1.0 copy-done.5
  107.9 4.5 fusion.98
  113.0 0.8 fusion.67
  114.2 0.6 dynamic-slice
  115.5 0.9 copy.339
  116.4 0.9 copy.341
  117.3 13.4 %reduce-scatter.16.cloned.1.call-done = f32[128,4]{1,0:T(8,128)} async-done(((f32[512,4]{1,0:T(8,128)}), f32[128,4]{1,0:T(8,128)}) %reduce-scatter.16.cloned.1.call-update) | async-done | bytes 2064
  130.7 0.9 copy.335
  131.6 21.7 %reduce-scatter.18.cloned.1.call-done = f32[128,4]{1,0:T(8,128)} async-done(((f32[512,4]{1,0:T(8,128)}), f32[128,4]{1,0:T(8,128)}) %reduce-scatter.18.cloned.1.call-update) | async-done | bytes 2064
  153.3 0.9 copy.337
  155.0 52.2 %all-reduce.11.cloned.1.call-done = (f32[512,4,128]{2,1,0:T(4,128)}, f32[512,4,128]{2,1,0:T(4,128)}) async-done(((f32[512,4,128]{2,1,0:T(4,128)}, f32[512,4,128]{2,1,0:T(4,128)}), (f32[512,4,128]{2,1,0:T(4,128)}, f32[512,4,128]{2,1,0:T(4,128)})) %all-reduce.11.cloned.1.call-update) | async-done | bytes 2097168
  207.1 3.3 fusion.41
  210.8 0.7 fusion.51
  211.6 1.1 convert_element_type.77
  212.8 1.4 scatter_custom_fusion.8
  214.2 76.7 %all-reduce.9.cloned.1.call-done = bf16[128,4096]{1,0:T(8,128)(2,1)} async-done(((bf16[128,4096]{1,0:T(8,128)(2,1)}), bf16[128,4096]{1,0:T(8,128)(2,1)}) %all-reduce.9.cloned.1.call-update) | async-done | bytes 1048592 | tf_op jit(solution)/shard_map/psum | solution.py:241
  291.0 1.5 multiply_reduce_fusion
  292.5 1.5 multiply_convert_fusion
  294.1 4.4 gather_fusion.13
  298.5 2.6 broadcast_select_fusion
  301.1 51.6 %all_to_all.10 = bf16[4,128,4096]{2,1,0:T(8,128)(2,1)} all-to-all(bf16[4,128,4096]{2,1,0:T(8,128)(2,1)S(1)} %broadcast_select_fusion), channel_id=1, replica_groups=mesh['dp'=4,'mp'=8] {'dp'}, dimensions={0} | all-to-all | bytes 8388608 | tf_op jit(solution)/shard_map/all_to_all | solution.py:264
  352.7 18.0 %fusion.19 = f32[2,4,2,64,1024]{4,3,0,1,2:T(8,128)} fusion(bf16[2,2,1024,4096]{3,2,1,0:T(8,128)(2,1)} %param.27, bf16[4,2,64,4096,1]{3,2,1,0,4:T(8,128)(2,1)} %bitcast.190), kind=kOutput, calls=%fused_computation.45 | convolution fusion | flops 8589934592 | bytes 41943040 | tf_op jit(solution)/shard_map/sjcd,jkfd->ksjcf/dot_general | solution.py:267
  370.7 13.6 %fusion.12 = bf16[4,2,64,4096]{3,2,0,1:T(8,128)(2,1)} fusion(bf16[2,1024,4096]{2,1,0:T(8,128)(2,1)} %param.28, f32[2,4,2,64,1024]{4,3,0,1,2:T(8,128)} %fusion.19), kind=kOutput, calls=%fused_computation.36 | convolution fusion | flops 4300210176 | bytes 25165824 | tf_op jit(solution)/shard_map/sjcf,jfd->sjcd/dot_general | solution.py:271
  385.5 86.1 %reduce-scatter.14.cloned.1.call-done = bf16[4,2,64,512]{3,2,0,1:T(8,128)(2,1)} async-done(((bf16[4,2,64,4096]{3,2,0,1:T(8,128)(2,1)}), bf16[4,2,64,512]{3,2,0,1:T(8,128)(2,1)}) %reduce-scatter.14.cloned.1.call-update) | async-done | bytes 524304 | tf_op jit(solution)/shard_map/reduce_scatter | solution.py:274
  471.7 1.9 copy.318
  473.5 3.6 all-to-all-start.1
  477.4 1.6 convert_element_type.78
  478.9 7.0 %all-to-all-done.1 = bf16[4,128,512]{2,1,0:T(8,128)(2,1)S(1)} async-done(((bf16[4,128,512]{2,1,0:T(8,128)(2,1)}), bf16[4,128,512]{2,1,0:T(8,128)(2,1)S(1)}, u32[]{:S(2)}, u32[]{:S(2)}) %all-to-all-start.1) | async-done | bytes 524320 | tf_op jit(solution)/shard_map/all_to_all | solution.py:277
  486.0 1.2 gather_fusion.14
  487.2 0.8 multiply_reduce_fusion.1
  488.1 1.6 add_convert_fusion
  (176 shorter events, 14.4 us)
Async XLA Ops:
  6.5 24.7 %copy-start = (bf16[128,4096]{1,0:T(8,128)(2,1)S(1)}, bf16[128,4096]{1,0:T(8,128)(2,1)}, u32[]{:S(2)}) copy-start(bf16[128,4096]{1,0:T(8,128)(2,1)} %param.21) | copy-start | bytes 3145732
  6.5 108.9 %reduce-scatter.20.cloned.1.call-start = ((), (), s32[]{:S(2)}) async-start(), calls=%async_computation.11 | async-start | bytes 327680
  22.6 7.9 %copy-start.12 = (s32[8,32]{1,0:T(8,128)S(1)}, s32[8,32]{1,0:T(8,128)}, u32[]{:S(2)}) copy-start(s32[8,32]{1,0:T(8,128)} %param.36) | copy-start | bytes 3076
  49.6 1.9 copy-start.2
  55.2 9.3 %copy-start.15 = (s32[32]{0:T(128)S(1)}, s32[32]{0:T(128)}, u32[]{:S(2)}) copy-start(s32[32]{0:T(128)} %param.35) | copy-start | bytes 388
  55.2 12.6 %copy-start.13 = (s32[32,4]{0,1:T(4,128)S(1)}, s32[32,4]{0,1:T(4,128)}, u32[]{:S(2)}) copy-start(s32[32,4]{0,1:T(4,128)} %param.37) | copy-start | bytes 1540
  55.2 13.4 %copy-start.11 = (s32[128,2]{0,1:T(2,128)S(1)}, s32[128,2]{0,1:T(2,128)}, u32[]{:S(2)}) copy-start(s32[128,2]{0,1:T(2,128)} %param.41) | copy-start | bytes 3076
  64.4 51.9 %reduce-scatter.22.cloned.1.call-start = ((), (), s32[]{:S(2)}) async-start(), calls=%async_computation.12 | async-start | bytes 327680
  74.2 1.7 copy-start.3
  80.0 50.7 %reduce-scatter.16.cloned.1.call-start = ((), (), s32[]{:S(2)}) async-start(), calls=%async_computation.9 | async-start | bytes 327680
  82.1 71.2 %reduce-scatter.18.cloned.1.call-start = ((), (), s32[]{:S(2)}) async-start(), calls=%async_computation.10 | async-start | bytes 327680
  84.1 123.0 %all-reduce.11.cloned.1.call-start = ((), (), s32[]{:S(2)}) async-start(), calls=%async_computation.13 | async-start | bytes 4194304
  91.3 16.6 %copy-start.14 = (s32[128]{0:T(128)S(1)}, s32[128]{0:T(128)}, u32[]{:S(2)}) copy-start(s32[128]{0:T(128)} %param.40) | copy-start | bytes 1540
  99.1 7.5 %copy-start.6 = (f32[512,4,128]{2,1,0:T(4,128)}, f32[512,4,128]{2,1,0:T(4,128)S(1)}, u32[]{:S(2)}) copy-start(f32[512,4,128]{2,1,0:T(4,128)S(1)} %scatter_fusion) | copy-start | bytes 3145732
  106.5 1.0 copy-start.5
  106.5 7.6 %copy-start.16 = (u32[32]{0:T(128)S(1)}, u32[32]{0:T(128)}, u32[]{:S(2)}) copy-start(u32[32]{0:T(128)} %constant.351) | copy-start | bytes 388
  107.5 183.4 %all-reduce.9.cloned.1.call-start = ((), (), s32[]{:S(2)}) async-start(), calls=%async_computation.7 | async-start | bytes 2097152 | tf_op jit(solution)/shard_map/psum | solution.py:241
  207.1 3.7 copy-start.7
  210.5 1.0 copy-start.8
  211.5 81.0 %copy-start.10 = (f32[4096]{0:T(1024)S(1)}, f32[4096]{0:T(1024)}, u32[]{:S(2)}) copy-start(f32[4096]{0:T(1024)} %param.25) | copy-start | bytes 49156
  212.7 258.9 %reduce-scatter.14.cloned.1.call-start = ((), (), s32[]{:S(2)}) async-start(), calls=%async_computation.8 | async-start | bytes 4718592 | tf_op jit(solution)/shard_map/reduce_scatter | solution.py:274
  384.3 0.8 copy-start.9
  384.3 93.0 %copy-start.4 = (bf16[128,4096]{1,0:T(8,128)(2,1)S(1)}, bf16[128,4096]{1,0:T(8,128)(2,1)}, u32[]{:S(2)}) copy-start(bf16[128,4096]{1,0:T(8,128)(2,1)} %all-reduce.9.cloned.1.call-done) | copy-start | bytes 3145732
  473.5 16.2 %copy-start.1 = (bf16[128,4096]{1,0:T(8,128)(2,1)S(1)}, bf16[128,4096]{1,0:T(8,128)(2,1)}, u32[]{:S(2)}) copy-start(bf16[128,4096]{1,0:T(8,128)(2,1)} %param.21) | copy-start | bytes 3145732
  473.5 12.4 %all-to-all-start.1 = ((bf16[4,128,512]{2,1,0:T(8,128)(2,1)}), bf16[4,128,512]{2,1,0:T(8,128)(2,1)S(1)}, u32[]{:S(2)}, u32[]{:S(2)}) async-start(bf16[4,128,512]{2,1,0:T(8,128)(2,1)} %bitcast.67), calls=%async_computation.2 | async-start | bytes 1048576 | tf_op jit(solution)/shard_map/all_to_all | solution.py:277
Sparse Core Ops, SparseCore 0:
  64.6 20.8 reduce-scatter.19
  88.1 20.0 reduce-scatter.21
  110.7 19.9 reduce-scatter.15
  133.2 20.0 reduce-scatter.17
  155.5 51.5 all-reduce.10
  212.9 78.0 all-reduce.8
  384.5 87.1 reduce-scatter.13
where the time goes:
time: 498 us; the launch traced here: 497 us
  waiting for transfers between devices  257 us (52%)
  local copies, waits for them, and re-layouts  70.3 us (14%)
  blocking collectives  60.2 us (12%)
  matrix products  51.1 us (10%)
  other arithmetic  38.7 us (8%)
  between operations  14.9 us (3%)
    unnamed x12, waiting for transfers between devices  87.4 us
    reduce_scatter x1, waiting for transfers between devices, shards(): lax.psum_scatter(expert_partial.astype(jnp.bfloat16), 'mp', scatter_dimen...  86.1 us
    psum x1, waiting for transfers between devices, shards(): hidden = lax.psum(projected.astype(jnp.bfloat16), 'mp').astype(jnp.float32)  76.7 us
    all_to_all x1, blocking collectives, shards(): lax.all_to_all(outgoing, 'dp', split_axis=0, concat_axis=0, tiled=True)  51.6 us
    dot_general x1, matrix products, shards(): jnp.einsum('sjcd,jkfd->ksjcf', incoming, expert_in, preferred_element_typ...  18 us
    scatter x2, local copies, waits for them, and re-layouts, spread_rows(): sum_rows = jnp.zeros((requests, groups, head_width), jnp.float32).at[flat...  14.6 us
    dot_general x1, matrix products, shards(): jnp.einsum('sjcf,jfd->sjcd', expert_hidden, expert_out, preferred_element...  13.6 us
    dot_general x3, matrix products, weigh_scores(): jnp.einsum(pattern, weights.astype(jnp.bfloat16), values, preferred_eleme...  10.1 us
  transfers between devices with their start and end apart: 8, of which 6 were waited for; matrix products, arithmetic and copies ran while one was open for 11% of the time, Pallas kernels for 0%

commit v1 on v0

--- a/solution.py
+++ b/solution.py
@@ -238,7 +238,9 @@
         jnp.float32
     )
     projected = lax.dynamic_update_slice_in_dim(projected, own_cols, start_col, 1)
-    hidden = lax.psum(projected.astype(jnp.bfloat16), "mp").astype(jnp.float32)
+    hidden = jnp.sum(lax.all_gather(projected.astype(jnp.bfloat16), "mp"), axis=0).astype(
+        jnp.float32
+    )
     inv_rms = lax.rsqrt(jnp.mean(hidden * hidden, axis=1) + NORM_EPS)
     normed = (hidden * inv_rms[:, None] * norm_gain[None, :]).astype(jnp.bfloat16)
     kept_cols = lax.dynamic_slice_in_dim(hidden, start_col, slice_width, 1)

time: 498 us -> 552 us (1.11); the launches traced: 497 us -> 545 us
  waiting for transfers between devices: 257 us -> 303 us
    all_gather x0 -> x1, waiting for transfers between devices: none -> 124 us  [shards(): lax.all_gather(projected.astype(jnp.bfloat16), 'mp')]
    psum x1 -> x0, waiting for transfers between devices: 76.7 us -> none  [shards(): hidden = lax.psum(projected.astype(jnp.bfloat16), 'mp').astype(jnp.float32)]
  transfers between devices with their start and end apart: 8 -> 8, of which waited for: 6 -> 6; matrix products, arithmetic and copies ran while one was open for 11% -> 10% of each run, Pallas kernels for 0% -> 0%
where the time goes in v1:
time: 552 us; the launch traced here: 545 us
  waiting for transfers between devices  303 us (55%)
  local copies, waits for them, and re-layouts  69.9 us (13%)
  blocking collectives  60.4 us (11%)
  matrix products  51.1 us (9%)
  other arithmetic  41.3 us (7%)
  between operations  15.1 us (3%)
    all_gather x1, waiting for transfers between devices, shards(): lax.all_gather(projected.astype(jnp.bfloat16), 'mp')  124 us
    unnamed x12, waiting for transfers between devices  87.2 us
    reduce_scatter x1, waiting for transfers between devices, shards(): lax.psum_scatter(expert_partial.astype(jnp.bfloat16), 'mp', scatter_dimen...  83.6 us
    all_to_all x1, blocking collectives, shards(): lax.all_to_all(outgoing, 'dp', split_axis=0, concat_axis=0, tiled=True)  51.8 us
    dot_general x1, matrix products, shards(): jnp.einsum('sjcd,jkfd->ksjcf', incoming, expert_in, preferred_element_typ...  18 us
    scatter x2, local copies, waits for them, and re-layouts, spread_rows(): sum_rows = jnp.zeros((requests, groups, head_width), jnp.float32).at[flat...  14.6 us
    dot_general x1, matrix products, shards(): jnp.einsum('sjcf,jfd->sjcd', expert_hidden, expert_out, preferred_element...  13.6 us
  transfers between devices with their start and end apart: 8, of which 6 were waited for; matrix products, arithmetic and copies ran while one was open for 10% of the time, Pallas kernels for 0%

profile of v1, /device:TPU:0, one launch (start us, length us, event | category | flops | bytes accessed | tf_op | source)
XLA Modules:
  0.0 545.0 jit_solution(1399629381164674452)
XLA Ops:
  6.5 0.7 fusion.84
  7.3 1.4 fusion.85
  8.8 0.6 scatter_custom_fusion
  9.6 2.3 sort.34
  12.0 0.7 shift-left_bitcast_fusion.1
  13.3 0.7 compare_select_fusion.11
  14.0 3.6 gather_fusion.1
  17.6 0.7 and_select_fusion.2
  18.8 3.8 sort.35
  22.6 6.9 %gather_fusion.2 = s32[1024]{0:T(1024)S(1)} fusion(s32[512]{0:T(512)S(1)} %get-tuple-element.8, s32[1024]{0:T(1024)S(1)} %broadcast_clamp_fusion), kind=kCustom, calls=%fused_computation.2 | custom fusion | bytes 12288 | tf_op jit(solution)/shard_map/jit(_take)/gather | solution.py:137
  31.3 8.6 %all_gather.9 = bf16[512,512]{1,0:T(8,128)(2,1)S(1)} all-gather(bf16[128,512]{1,0:T(8,128)(2,1)S(1)} %constant_dynamic-slice_fusion), channel_id=1, replica_groups=mesh['dp'=4,'mp'=8] {'dp'}, dimensions={0}, use_global_device_ids=true | all-gather | bytes 655360 | tf_op jit(solution)/shard_map/all_gather | solution.py:126
  40.0 1.0 gather_fusion.5
  41.1 5.8 %gather_fusion.7 = bf16[64,2,128,128]{3,2,1,0:T(8,128)(2,1)} fusion(bf16[2,96,128,128]{3,2,1,0:T(8,128)(2,1)} %bitcast.190, s32[1024]{0:T(1024)S(1)} %pad_clamp_fusion.5), kind=kCustom, calls=%fused_computation.7 | custom fusion | bytes 8388864 | tf_op jit(solution)/shard_map/vmap(jit(_take))/gather | solution.py:48
  46.9 2.6 fusion.18
  49.6 1.8 fusion.96
  51.5 0.6 gather_fusion.4
  52.2 3.0 fusion.4
  55.2 7.2 %fusion.5 = (f32[2,128,4]{1,2,0:T(4,128)S(1)}, bf16[2,128,4,4096]{3,1,2,0:T(8,128)(2,1)}) fusion(f32[2,128,4,4096]{3,1,2,0:T(8,128)S(1)} %get-tuple-element.35, f32[2,128,4]{1,2,0:T(4,128)S(1)} %get-tuple-element.34, pred[2,4096]{1,0:T(4,128)(4,1)S(1)} %broadcast_compare_fusion), kind=kLoop, calls=%fused_computation.31 | loop fusion | flops 25164800 | bytes 25182208 | tf_op jit(solution)/shard_map/vmap()/reduce_sum | solution.py:37
  62.6 1.8 scatter_custom_fusion.6
  64.5 0.6 fusion.87
  65.4 1.0 scatter_custom_fusion.3
  66.6 0.7 shift-left_bitcast_fusion
  67.3 0.6 gather_fusion.8
  69.2 1.0 gather_fusion.10
  70.4 3.8 gather_fusion.12
  76.0 0.6 gather_fusion.9
  76.7 0.6 fusion.27
  77.3 0.8 fusion.28
  78.3 1.8 scatter_custom_fusion.7
  80.3 1.8 scatter_custom_fusion.2
  82.3 1.8 scatter_custom_fusion.4
  84.2 6.3 %fusion.7 = f32[2,128,4,128]{3,1,0,2:T(8,128)S(1)} fusion(bf16[2,4096,128,1]{2,1,0,3:T(8,128)(2,1)} %bitcast.196, bf16[2,128,4,4096]{3,1,2,0:T(8,128)(2,1)} %get-tuple-element.23), kind=kOutput, calls=%fused_computation.33 | convolution fusion | flops 1073741824 | bytes 11010048 | tf_op jit(solution)/shard_map/vmap(sgl,ld->sgd)/dot_general | solution.py:38
  91.8 7.3 %scatter_fusion = f32[512,4,128]{2,1,0:T(4,128)S(1)} fusion(f32[512,4,128]{2,1,0:T(4,128)S(1)} %broadcast.675.clone.1, s32[256]{0:T(256)S(1)} %bitcast.215, f32[256,4,128]{2,1,0:T(4,128)S(1)} %copy.278), kind=kCustom, calls=%fused_computation.16 | custom fusion | bytes 1573888 | tf_op jit(solution)/shard_map/scatter | solution.py:71
  99.3 7.3 %scatter_fusion.1 = f32[512,4,128]{2,1,0:T(4,128)S(1)} fusion(f32[512,4,128]{2,1,0:T(4,128)S(1)} %broadcast.675.clone, s32[256]{0:T(256)S(1)} %bitcast.212, f32[256,4,128]{2,1,0:T(4,128)S(1)} %copy.293), kind=kCustom, calls=%fused_computation.20 | custom fusion | bytes 1573888 | tf_op jit(solution)/shard_map/scatter | solution.py:71
  106.6 1.0 copy-done.6
  108.3 4.5 fusion.98
  113.3 0.8 fusion.67
  114.5 0.6 dynamic-slice
  115.8 0.9 copy.339
  116.7 0.9 copy.341
  117.6 13.2 %reduce-scatter.16.cloned.1.call-done = f32[128,4]{1,0:T(8,128)} async-done(((f32[512,4]{1,0:T(8,128)}), f32[128,4]{1,0:T(8,128)}) %reduce-scatter.16.cloned.1.call-update) | async-done | bytes 2064
  130.8 0.9 copy.335
  131.7 21.6 %reduce-scatter.18.cloned.1.call-done = f32[128,4]{1,0:T(8,128)} async-done(((f32[512,4]{1,0:T(8,128)}), f32[128,4]{1,0:T(8,128)}) %reduce-scatter.18.cloned.1.call-update) | async-done | bytes 2064
  153.3 0.9 copy.337
  155.1 52.2 %all-reduce.8.cloned.1.call-done = (f32[512,4,128]{2,1,0:T(4,128)}, f32[512,4,128]{2,1,0:T(4,128)}) async-done(((f32[512,4,128]{2,1,0:T(4,128)}, f32[512,4,128]{2,1,0:T(4,128)}), (f32[512,4,128]{2,1,0:T(4,128)}, f32[512,4,128]{2,1,0:T(4,128)})) %all-reduce.8.cloned.1.call-update) | async-done | bytes 2097168
  207.3 3.3 fusion.41
  210.9 0.7 fusion.51
  211.7 1.2 convert_element_type.79
  213.0 1.4 scatter_custom_fusion.8
  214.4 123.7 %all-gather.3.cloned.1.call-done = bf16[1024,4096]{1,0:T(8,128)(2,1)} async-done(((bf16[128,4096]{1,0:T(8,128)(2,1)}), bf16[1024,4096]{1,0:T(8,128)(2,1)}) %all-gather.3.cloned.1.call-update) | async-done | bytes 8388624 | tf_op jit(solution)/shard_map/all_gather | solution.py:241
  338.1 4.9 reduce_sum.121
  343.8 4.4 gather_fusion.13
  348.1 2.6 broadcast_select_fusion
  350.8 51.8 %all_to_all.10 = bf16[4,128,4096]{2,1,0:T(8,128)(2,1)} all-to-all(bf16[4,128,4096]{2,1,0:T(8,128)(2,1)S(1)} %broadcast_select_fusion), channel_id=1, replica_groups=mesh['dp'=4,'mp'=8] {'dp'}, dimensions={0} | all-to-all | bytes 8388608 | tf_op jit(solution)/shard_map/all_to_all | solution.py:266
  402.5 18.0 %fusion.19 = f32[2,4,2,64,1024]{4,3,0,1,2:T(8,128)} fusion(bf16[2,2,1024,4096]{3,2,1,0:T(8,128)(2,1)} %param.27, bf16[4,2,64,4096,1]{3,2,1,0,4:T(8,128)(2,1)} %bitcast.192), kind=kOutput, calls=%fused_computation.45 | convolution fusion | flops 8589934592 | bytes 41943040 | tf_op jit(solution)/shard_map/sjcd,jkfd->ksjcf/dot_general | solution.py:269
  420.5 13.6 %fusion.12 = bf16[4,2,64,4096]{3,2,0,1:T(8,128)(2,1)} fusion(bf16[2,1024,4096]{2,1,0:T(8,128)(2,1)} %param.28, f32[2,4,2,64,1024]{4,3,0,1,2:T(8,128)} %fusion.19), kind=kOutput, calls=%fused_computation.36 | convolution fusion | flops 4300210176 | bytes 25165824 | tf_op jit(solution)/shard_map/sjcf,jfd->sjcd/dot_general | solution.py:273
  434.5 1.5 convert_element_type.80
  436.5 83.6 %reduce-scatter.14.cloned.1.call-done = bf16[4,2,64,512]{3,2,0,1:T(8,128)(2,1)} async-done(((bf16[4,2,64,4096]{3,2,0,1:T(8,128)(2,1)}), bf16[4,2,64,512]{3,2,0,1:T(8,128)(2,1)}) %reduce-scatter.14.cloned.1.call-update) | async-done | bytes 524304 | tf_op jit(solution)/shard_map/reduce_scatter | solution.py:276
  520.0 1.9 copy.318
  521.9 3.5 all-to-all-start.1
  525.6 8.6 %all-to-all-done.1 = bf16[4,128,512]{2,1,0:T(8,128)(2,1)S(1)} async-done(((bf16[4,128,512]{2,1,0:T(8,128)(2,1)}), bf16[4,128,512]{2,1,0:T(8,128)(2,1)S(1)}, u32[]{:S(2)}, u32[]{:S(2)}) %all-to-all-start.1) | async-done | bytes 524320 | tf_op jit(solution)/shard_map/all_to_all | solution.py:279
  534.2 1.2 gather_fusion.14
  535.4 0.8 multiply_reduce_fusion.1
  536.3 1.6 add_convert_fusion
  (179 shorter events, 14.3 us)
Async XLA Ops:
  6.5 24.7 %copy-start = (bf16[128,4096]{1,0:T(8,128)(2,1)S(1)}, bf16[128,4096]{1,0:T(8,128)(2,1)}, u32[]{:S(2)}) copy-start(bf16[128,4096]{1,0:T(8,128)(2,1)} %param.21) | copy-start | bytes 3145732
  6.5 109.2 %reduce-scatter.20.cloned.1.call-start = ((), (), s32[]{:S(2)}) async-start(), calls=%async_computation.11 | async-start | bytes 327680
  22.6 7.9 %copy-start.13 = (s32[8,32]{1,0:T(8,128)S(1)}, s32[8,32]{1,0:T(8,128)}, u32[]{:S(2)}) copy-start(s32[8,32]{1,0:T(8,128)} %param.36) | copy-start | bytes 3076
  49.6 1.9 copy-start.2
  55.2 9.3 %copy-start.16 = (s32[32]{0:T(128)S(1)}, s32[32]{0:T(128)}, u32[]{:S(2)}) copy-start(s32[32]{0:T(128)} %param.35) | copy-start | bytes 388
  55.2 12.7 %copy-start.14 = (s32[32,4]{0,1:T(4,128)S(1)}, s32[32,4]{0,1:T(4,128)}, u32[]{:S(2)}) copy-start(s32[32,4]{0,1:T(4,128)} %param.37) | copy-start | bytes 1540
  55.2 13.5 %copy-start.12 = (s32[128,2]{0,1:T(2,128)S(1)}, s32[128,2]{0,1:T(2,128)}, u32[]{:S(2)}) copy-start(s32[128,2]{0,1:T(2,128)} %param.41) | copy-start | bytes 3076
  64.4 52.2 %reduce-scatter.22.cloned.1.call-start = ((), (), s32[]{:S(2)}) async-start(), calls=%async_computation.12 | async-start | bytes 327680
  74.2 1.7 copy-start.3
  80.1 50.7 %reduce-scatter.16.cloned.1.call-start = ((), (), s32[]{:S(2)}) async-start(), calls=%async_computation.9 | async-start | bytes 327680
  82.2 71.2 %reduce-scatter.18.cloned.1.call-start = ((), (), s32[]{:S(2)}) async-start(), calls=%async_computation.10 | async-start | bytes 327680
  84.2 123.1 %all-reduce.8.cloned.1.call-start = ((), (), s32[]{:S(2)}) async-start(), calls=%async_computation.13 | async-start | bytes 4194304
  91.3 16.8 %copy-start.15 = (s32[128]{0:T(128)S(1)}, s32[128]{0:T(128)}, u32[]{:S(2)}) copy-start(s32[128]{0:T(128)} %param.40) | copy-start | bytes 1540
  99.1 7.5 %copy-start.7 = (f32[512,4,128]{2,1,0:T(4,128)}, f32[512,4,128]{2,1,0:T(4,128)S(1)}, u32[]{:S(2)}) copy-start(f32[512,4,128]{2,1,0:T(4,128)S(1)} %scatter_fusion) | copy-start | bytes 3145732
  106.6 1.0 copy-start.6
  106.6 7.9 %copy-start.17 = (u32[32]{0:T(128)S(1)}, u32[32]{0:T(128)}, u32[]{:S(2)}) copy-start(u32[32]{0:T(128)} %constant.352) | copy-start | bytes 388
  107.6 230.5 %all-gather.3.cloned.1.call-start = ((), (), s32[]{:S(2)}) async-start(), calls=%async_computation.8 | async-start | bytes 9437184 | tf_op jit(solution)/shard_map/all_gather | solution.py:241
  207.3 3.7 copy-start.8
  210.6 1.0 copy-start.9
  212.9 307.1 %reduce-scatter.14.cloned.1.call-start = ((), (), s32[]{:S(2)}) async-start(), calls=%async_computation.7 | async-start | bytes 4718592 | tf_op jit(solution)/shard_map/reduce_scatter | solution.py:276
  338.1 5.2 copy-start.11
  343.7 4.5 copy-start.4
  434.1 2.0 copy-start.5
  434.1 2.0 copy-start.10
  434.5 103.4 %copy-start.1 = (bf16[128,4096]{1,0:T(8,128)(2,1)S(1)}, bf16[128,4096]{1,0:T(8,128)(2,1)}, u32[]{:S(2)}) copy-start(bf16[128,4096]{1,0:T(8,128)(2,1)} %param.21) | copy-start | bytes 3145732
  521.9 12.3 %all-to-all-start.1 = ((bf16[4,128,512]{2,1,0:T(8,128)(2,1)}), bf16[4,128,512]{2,1,0:T(8,128)(2,1)S(1)}, u32[]{:S(2)}, u32[]{:S(2)}) async-start(bf16[4,128,512]{2,1,0:T(8,128)(2,1)} %bitcast.68), calls=%async_computation.2 | async-start | bytes 1048576 | tf_op jit(solution)/shard_map/all_to_all | solution.py:279
Sparse Core Ops, SparseCore 0:
  64.6 20.9 reduce-scatter.19
  88.1 20.0 reduce-scatter.21
  110.7 20.0 reduce-scatter.15
  133.3 20.0 reduce-scatter.17
  155.6 51.5 all-reduce.7
  213.0 124.9 all-gather.2
  434.3 85.7 reduce-scatter.13
